TPU v7x, 32 devices: a whole 2x2x4 slice. The times are simulated.
32 devices in a mesh: groups: 2 (over x), tm: 16 (over z, y, core).
Axes of the slice: x: 2, y: 2, z: 4, core: 2. Of those that a mesh axis runs over, the one named last changes fastest.
Arguments:
- observed: float32 [32, 128], P(('groups', 'tm')), parts along dimension 0, may hold values from -6 to 6
- obs_masks: int32 [32, 128], P(('groups', 'tm')), parts along dimension 0, may hold values 0 or 1
- decay_rates: float32 [256], P('groups'), parts along dimension 0, may hold values from 0.05 to 0.5
- noise_var: float32 [256], P('groups'), parts along dimension 0, may hold values from 0.05 to 0.5
- spatial_cov: float32 [256, 128], P('groups'), parts along dimension 0, may hold values from -1 to 4, as said below
Outputs:
- smooth_mean: float32 [32, 256], P(('groups', 'tm')), parts along dimension 0
- smooth_cov: float32 [32, 256, 256], P(('groups', 'tm')), parts along dimension 0
There are 2 independent parts, one for each index of `groups`. A program takes and returns all parts, laid end to end along the dimension named above; each array names one. Nothing has to cross between parts.
Inputs may be any that keep to these rules, and one draw needn't show every extreme that they name: spatial_cov is symmetric, and each diagonal entry is positive and larger than the sum of the magnitudes of the other entries of its row.
All inputs are finite; a program needn't handle non-finite values. No bound on the sum of `obs_masks` on one device may be relied on, other than what follows from the above.
Results may differ from a plain program's by a relative error of at most 0.0003.
Values sent between devices are 32-bit elements; how exact they have to be, the bound alone decides.
No kernel may reach another device: no remote copies, remote signals or barrier semaphores. Data moves between devices by JAX's collectives and lax.ppermute only.
A program may use at most 128 MiB of HBM per device.

v0:
```python
import jax
import jax.numpy as jnp
from jax import lax
from jax.sharding import PartitionSpec as P

HIGHEST = lax.Precision.HIGHEST
JITTER = 0.001


def matmul_hi(left, right):
    return jnp.matmul(left, right, precision=HIGHEST)


def swap_last(matrix):
    return jnp.swapaxes(matrix, -1, -2)


def apply_trans(transit, matrix):
    points = transit.shape[1]
    upper_half = matrix[..., :points, :]
    lower_half = matrix[..., points:, :]
    return jnp.concatenate(
        [
            transit[0][:, None] * upper_half + transit[1][:, None] * lower_half,
            transit[2][:, None] * upper_half + transit[3][:, None] * lower_half,
        ],
        axis=-2,
    )


def build_model(decay_rates, spatial_cov):
    decay_one = jnp.exp(-decay_rates)
    transit = jnp.stack(
        [
            decay_one * (1.0 + decay_rates),
            decay_one * decay_rates,
            -decay_one * decay_rates,
            decay_one * (1.0 - decay_rates),
        ]
    )
    decay_two = jnp.exp(-2.0 * decay_rates)
    var_ff = 1.0 - decay_two * (1.0 + 2.0 * decay_rates + 2.0 * decay_rates * decay_rates)
    cov_fg = 2.0 * decay_rates * decay_rates * decay_two
    var_gg = 1.0 - decay_two * (1.0 - 2.0 * decay_rates + 2.0 * decay_rates * decay_rates)
    fac_ff = jnp.sqrt(var_ff)
    fac_gf = cov_fg / fac_ff
    fac_gg = jnp.sqrt(var_gg - fac_gf * fac_gf)

    def scaled(left, right):
        return left[:, None] * spatial_cov * right[None, :]

    zero_block = jnp.zeros_like(spatial_cov)
    process = jnp.block(
        [
            [scaled(fac_ff, fac_ff), scaled(fac_ff, fac_gf)],
            [scaled(fac_gf, fac_ff), scaled(fac_gf, fac_gf) + scaled(fac_gg, fac_gg)],
        ]
    )
    process = process + JITTER * jnp.eye(2 * spatial_cov.shape[0], dtype=jnp.float32)
    prior = jnp.block([[spatial_cov, zero_block], [zero_block, spatial_cov]])
    return (transit, process, prior)


def predict(transit, process, mean, cov):
    forward_cov = apply_trans(transit, cov)
    cov_pred = apply_trans(transit, swap_last(forward_cov)) + process
    mean_pred = apply_trans(transit, mean[:, None])[:, 0]
    return (mean_pred, cov_pred)


def kalman_update(mean_pred, cov_pred, obs, root):
    points = obs.shape[-1]
    normal = (
        jnp.eye(points, dtype=jnp.float32)
        + root[:, None] * cov_pred[:points, :points] * root[None, :]
    )
    factor = jnp.linalg.cholesky(normal)
    innovation = root * (obs - mean_pred[:points])
    rhs = jnp.concatenate([root[:, None] * cov_pred[:points, :], innovation[:, None]], axis=1)
    half = lax.linalg.triangular_solve(factor, rhs, left_side=True, lower=True)
    gain_half = half[:, :-1]
    cov_new = cov_pred - matmul_hi(swap_last(gain_half), gain_half)
    mean_new = mean_pred + matmul_hi(swap_last(gain_half), half[:, -1])
    return (mean_new, cov_new)


def smoother_elements(means, covs, last_flag, transit, process):
    forward_cov = apply_trans(transit, covs)
    predicted = apply_trans(transit, swap_last(forward_cov)) + process
    factor = jnp.linalg.cholesky(predicted)
    half_solve = lax.linalg.triangular_solve(factor, forward_cov, left_side=True, lower=True)
    gain_t = lax.linalg.triangular_solve(
        factor, half_solve, left_side=True, lower=True, transpose_a=True
    )
    gains = swap_last(gain_t) * (1.0 - last_flag.astype(jnp.float32))[:, None, None]
    forward_mean = apply_trans(transit, means[..., None])
    shift_means = means - matmul_hi(gains, forward_mean)[..., 0]
    shift_covs = covs - matmul_hi(gains, forward_cov)
    return (gains, shift_means, shift_covs)


def smooth_join(lower_el, higher_el):
    gain_a, mean_a, cov_a = lower_el
    gain_b, mean_b, cov_b = higher_el
    return (
        matmul_hi(gain_a, gain_b),
        matmul_hi(gain_a, mean_b[..., None])[..., 0] + mean_a,
        matmul_hi(matmul_hi(gain_a, cov_b), swap_last(gain_a)) + cov_a,
    )


def shards(observed, obs_masks, decay_rates, noise_var, spatial_cov):
    transit, process, prior = build_model(decay_rates, spatial_cov)
    local_steps, points = observed.shape
    width = 2 * points
    position = lax.axis_index("tm")
    tm_count = lax.axis_size("tm")
    total_steps = tm_count * local_steps
    root_local = jnp.sqrt(obs_masks.astype(jnp.float32) / noise_var)
    packed = jnp.stack([observed, root_local], axis=1)
    gathered = lax.all_gather(packed, "tm", tiled=True)
    obs_all = gathered[:, 0]
    root_all = gathered[:, 1]
    mean_first, cov_first = kalman_update(
        jnp.zeros((width,), jnp.float32), prior, obs_all[0], root_all[0]
    )
    last_local = position * local_steps + (local_steps - 1)

    def filter_step(step, mean, cov):
        mean_pred, cov_pred = predict(transit, process, mean, cov)
        obs_now = lax.dynamic_index_in_dim(obs_all, step, keepdims=False)
        root_now = lax.dynamic_index_in_dim(root_all, step, keepdims=False)
        return kalman_update(mean_pred, cov_pred, obs_now, root_now)

    if local_steps == 1:

        def body(step, carry):
            return filter_step(step, carry[0], carry[1])

        mean_last, cov_last = lax.fori_loop(1, last_local + 1, body, (mean_first, cov_first))
        means = mean_last[None]
        covs = cov_last[None]
    else:
        mean_buf = jnp.zeros((local_steps, width), jnp.float32).at[0].set(mean_first)
        cov_buf = jnp.zeros((local_steps, width, width), jnp.float32).at[0].set(cov_first)

        def body(step, carry):
            mean, cov, mean_buf, cov_buf = carry
            mean, cov = filter_step(step, mean, cov)
            slot = step % local_steps
            mean_buf = lax.dynamic_update_index_in_dim(mean_buf, mean, slot, 0)
            cov_buf = lax.dynamic_update_index_in_dim(cov_buf, cov, slot, 0)
            return (mean, cov, mean_buf, cov_buf)

        _, _, means, covs = lax.fori_loop(
            1, last_local + 1, body, (mean_first, cov_first, mean_buf, cov_buf)
        )
    global_step = position * local_steps + jnp.arange(local_steps)
    last_flag = global_step == total_steps - 1
    if local_steps == 1:

        def compute_elements(operand):
            return smoother_elements(operand[0], operand[1], last_flag, transit, process)

        def final_elements(operand):
            return (jnp.zeros_like(operand[1]), operand[0], operand[1])

        smooth = lax.cond(position == tm_count - 1, final_elements, compute_elements, (means, covs))
    else:
        smooth = smoother_elements(means, covs, last_flag, transit, process)
    if local_steps > 1:
        last_el = jax.tree.map(lambda leaf: leaf[-1], smooth)
        front_els = jax.tree.map(lambda leaf: leaf[:-1], smooth)

        def backward(running, element):
            joined = smooth_join(element, running)
            return (joined, joined)

        _, head_els = lax.scan(backward, last_el, front_els, reverse=True)
        suffixes = jax.tree.map(
            lambda head_leaf, last_leaf: jnp.concatenate([head_leaf, last_leaf[None]], axis=0),
            head_els,
            last_el,
        )
        block_total = jax.tree.map(lambda leaf: leaf[0], suffixes)
    else:
        block_total = jax.tree.map(lambda leaf: leaf[0], smooth)
    running = block_total
    shift = 1
    while shift < tm_count:
        pairs = [(source, source - shift) for source in range(shift, tm_count)]
        received = lax.ppermute(running, "tm", pairs)
        running = smooth_join(running, received)
        shift *= 2
    if local_steps == 1:
        return (running[1][None], running[2][None])
    pairs = [(source, source - 1) for source in range(1, tm_count)]
    after_mine = lax.ppermute(running, "tm", pairs)
    gains, shift_means, shift_covs = suffixes
    smooth_mean = matmul_hi(gains, after_mine[1][:, None])[..., 0] + shift_means
    smooth_cov = matmul_hi(matmul_hi(gains, after_mine[2]), swap_last(gains)) + shift_covs
    return (smooth_mean, smooth_cov)


def solution(mesh):
    placed = (
        P(("groups", "tm"), None),
        P(("groups", "tm"), None),
        P("groups"),
        P("groups"),
        P("groups", None),
    )
    return jax.shard_map(
        shards,
        mesh=mesh,
        in_specs=placed,
        out_specs=(P(("groups", "tm"), None), P(("groups", "tm"), None, None)),
        check_vma=False,
    )
```

profile of v0, /device:TPU:1, one launch (start us, length us, event | category | flops | bytes accessed | tf_op | source)
XLA Modules:
  0.0 498.3 jit_solution(2744481612989866936)
XLA Ops:
  0.7 0.6 copy-done.3
  1.3 0.7 copy-done.1
  2.0 23.1 %all_gather.3 = f32[16,2,128]{2,1,0:T(2,128)S(1)} all-gather(f32[1,2,128]{2,1,0:T(2,128)S(1)} %pad_maximum_fusion.3), channel_id=1, replica_groups=mesh['groups'=2,'tm'=16] {'tm'}, dimensions={0}, use_global_device_ids=true | all-gather | bytes 17408 | tf_op jit(solution)/shard_map/all_gather | solution.py:121
  25.7 11.7 %custom-call.32 = f32[128,128]{1,0:T(8,128)S(1)} custom-call(f32[128,128]{1,0:T(8,128)S(1)} %fusion.49), custom_call_target="Cholesky" | custom-call | tf_op jit(solution)/shard_map/jit(cholesky)/cholesky/custom-call.1 | solution.py:77
  37.5 0.7 compare_reduce_fusion.3
  38.2 0.6 fusion.47
  38.8 9.8 %custom-call.33 = f32[1,128,128]{1,2,0:T(8,128)S(1)} custom-call(f32[1,128,128]{2,1,0:T(8,128)S(1)} %fusion.47), custom_call_target="InvertDiagBlocksLowerTriangular" | custom-call | tf_op jit(solution)/shard_map/triangular_solve/custom-call.0 | solution.py:80
  49.9 24.9 %while.14 = (s32[]{:T(128)}, f32[256]{0:T(256)S(1)}, f32[256,256]{0,1:T(8,128)S(1)}, s32[]{:T(128)}, f32[128]{0:T(128)S(1)}, /*index=5*/f32[128]{0:T(128)S(1)}, ...) while((s32[]{:T(128)}, f32[256]{0:T(256)S(1)}, ...), condition=%wide.region_3.6_spmd, body=%wide.region_2.5_spmd.sunk | while | flops 152618752 | bytes 5461689 | solution.py:140
  51.0 11.7 %custom-call.37 = f32[128,128]{1,0:T(8,128)S(1)} custom-call(f32[128,128]{1,0:T(8,128)S(1)} %fusion.129), custom_call_target="Cholesky" | custom-call | tf_op jit(solution)/shard_map/while/body/jit(cholesky)/cholesky/custom-call.1 | solution.py:77
  62.7 0.7 compare_reduce_fusion.5
  63.4 0.6 fusion.130
  64.0 9.8 %custom-call.38 = f32[1,128,128]{1,2,0:T(8,128)S(1)} custom-call(f32[1,128,128]{2,1,0:T(8,128)S(1)} %fusion.130), custom_call_target="InvertDiagBlocksLowerTriangular" | custom-call | tf_op jit(solution)/shard_map/while/body/triangular_solve/custom-call.0 | solution.py:80
  74.9 63.7 %conditional.1 = (f32[1,256]{1,0:T(1,128)S(1)}, f32[256,256]{0,1:T(8,128)S(1)}, f32[1,256,256]{2,1,0:T(8,128)S(1)}) conditional(s32[]{:T(128)} %convert_element_type.18, (f32[128]{0:T(128)S(1)}, f32[1,256,256]{1,2,0:T(8,128)S(1)}, f32[128]{0:T(128)S(1)}, f32[128]{0:T(128)S(1)}, f32[128]{0:T(128)S(1)}, /*index=5*/f32[256,256]{0,1:T(8,128)S(1)}, ...), branch_computations={%region_4.11_spmd, %region_9.12_spmd} | conditional | flops 556025344 | bytes 11482373 | solution.py:168
  76.0 11.7 %custom-call.24 = f32[1,128,128]{2,1,0:T(8,128)S(1)} custom-call(f32[1,128,128]{2,1,0:T(8,128)S(1)} %cholesky.48), custom_call_target="Cholesky" | custom-call | tf_op jit(solution)/shard_map/cond/branch_0_fun/jit(cholesky)/cholesky | solution.py:90
  87.7 9.8 %custom-call.25 = f32[1,1,128,128]{2,3,1,0:T(8,128)S(1)} custom-call(f32[1,1,128,128]{3,2,1,0:T(8,128)S(1)} %get-tuple-element.221), custom_call_target="InvertDiagBlocksLowerTriangular" | custom-call | tf_op jit(solution)/shard_map/cond/branch_0_fun/jit(cholesky)/cholesky | solution.py:90
  98.0 11.7 %custom-call.26 = f32[1,128,128]{2,1,0:T(8,128)S(1)} custom-call(f32[1,128,128]{2,1,0:T(8,128)S(1)} %fusion.20), custom_call_target="Cholesky" | custom-call | tf_op jit(solution)/shard_map/cond/branch_0_fun/jit(cholesky)/cholesky | solution.py:90
  109.8 0.7 compare_reduce_fusion.1
  111.8 4.0 while.13
  111.9 0.6 fusion.133
  112.5 1.3 bitcast_dynamic-update-slice_fusion.3
  113.8 0.6 fusion.133
  114.4 1.3 bitcast_dynamic-update-slice_fusion.3
  115.7 19.7 %custom-call.27 = f32[1,2,128,128]{2,3,1,0:T(8,128)S(1)} custom-call(f32[1,2,128,128]{3,2,1,0:T(8,128)S(1)} %bitcast.262), custom_call_target="InvertDiagBlocksLowerTriangular" | custom-call | tf_op jit(solution)/shard_map/cond/branch_0_fun/triangular_solve | solution.py:92
  137.7 0.6 fusion.17
  138.6 1.9 collective-permute-start.7
  140.5 1.9 collective-permute-start.3
  142.4 1.9 collective-permute-start
  144.3 22.5 %collective-permute-done.3 = f32[256]{0:T(256)S(1)} collective-permute-done((f32[256]{0:T(256)S(1)}, f32[256]{0:T(256)S(1)}, u32[]{:S(2)}, u32[]{:S(2)}) %collective-permute-start.3) | collective-permute-done | bytes 1056 | tf_op jit(solution)/shard_map/ppermute | solution.py:192
  167.0 1.3 collective-permute-start.4
  168.4 0.6 fusion.65
  169.4 1.3 collective-permute-start.8
  170.7 0.6 fusion.59
  171.3 1.3 collective-permute-start.1
  172.6 48.7 %collective-permute-done.4 = f32[256]{0:T(256)S(1)} collective-permute-done((f32[256]{0:T(256)S(1)}, f32[256]{0:T(256)S(1)}, u32[]{:S(2)}, u32[]{:S(2)}) %collective-permute-start.4) | collective-permute-done | bytes 1056 | tf_op jit(solution)/shard_map/ppermute | solution.py:192
  221.6 1.3 collective-permute-start.5
  222.9 4.1 collective-permute-done.8
  227.8 1.3 collective-permute-start.9
  229.1 0.7 collective-permute-done.1
  230.2 1.3 collective-permute-start.2
  231.5 89.9 %collective-permute-done.5 = f32[256]{0:T(256)S(1)} collective-permute-done((f32[256]{0:T(256)S(1)}, f32[256]{0:T(256)S(1)}, u32[]{:S(2)}, u32[]{:S(2)}) %collective-permute-start.5) | collective-permute-done | bytes 1056 | tf_op jit(solution)/shard_map/ppermute | solution.py:192
  321.7 1.3 collective-permute-start.6
  323.1 7.4 %collective-permute-done.9 = f32[256,256]{1,0:T(8,128)S(1)} collective-permute-done((f32[256,256]{1,0:T(8,128)S(1)}, f32[256,256]{1,0:T(8,128)S(1)}, u32[]{:S(2)}, u32[]{:S(2)}) %collective-permute-start.9) | collective-permute-done | bytes 262176 | tf_op jit(solution)/shard_map/ppermute | solution.py:192
  331.3 1.3 collective-permute-start.10
  332.6 0.7 collective-permute-done.2
  333.7 145.0 %collective-permute-done.6 = f32[256]{0:T(256)S(1)} collective-permute-done((f32[256]{0:T(256)S(1)}, f32[256]{0:T(256)S(1)}, u32[]{:S(2)}, u32[]{:S(2)}) %collective-permute-start.6) | collective-permute-done | bytes 1056 | tf_op jit(solution)/shard_map/ppermute | solution.py:192
  478.7 0.9 convolution_add_fusion.4
  479.6 17.0 %collective-permute-done.10 = f32[256,256]{1,0:T(8,128)S(1)} collective-permute-done((f32[256,256]{1,0:T(8,128)S(1)}, f32[256,256]{1,0:T(8,128)S(1)}, u32[]{:S(2)}, u32[]{:S(2)}) %collective-permute-start.10) | collective-permute-done | bytes 262176 | tf_op jit(solution)/shard_map/ppermute | solution.py:192
  496.9 1.1 fusion.38
  (91 shorter events, 10.8 us)
Async XLA Ops:
  0.6 0.7 copy-start.3
  0.6 0.7 copy-start.4
  1.3 0.7 copy-start.1
  2.0 23.2 %copy-start.2 = (f32[128]{0:T(128)S(1)}, f32[128]{0:T(128)}, u32[]{:S(2)}) copy-start(f32[128]{0:T(128)} %param.14) | copy-start | bytes 1540
  2.0 23.3 %copy-start = (f32[128,128]{1,0:T(8,128)S(1)}, f32[128,128]{1,0:T(8,128)}, u32[]{:S(2)}) copy-start(f32[128,128]{1,0:T(8,128)} %param.16) | copy-start | bytes 196612
  138.6 29.8 %collective-permute-start.7 = (f32[256,256]{1,0:T(8,128)S(1)}, f32[256,256]{1,0:T(8,128)S(1)}, u32[]{:S(2)}, u32[]{:S(2)}) collective-permute-start(f32[256,256]{1,0:T(8,128)S(1)} %bitcast.242), channel_id=1, source_target_pairs={{1,0},{2,1},{3,2},{4,3},{5,4},{6,5},{7,6},{8,7},{9,8},{10,9},{11,1... | collective-permute-start | bytes 786440 | tf_op jit(solution)/shard_map/ppermute | solution.py:192
  140.5 26.3 %collective-permute-start.3 = (f32[256]{0:T(256)S(1)}, f32[256]{0:T(256)S(1)}, u32[]{:S(2)}, u32[]{:S(2)}) collective-permute-start(f32[256]{0:T(256)S(1)} %bitcast.255), channel_id=1, source_target_pairs={{1,0},{2,1},{3,2},{4,3},{5,4},{6,5},{7,6},{8,7},{9,8},{10,9},{11,1... | collective-permute-start | bytes 3080 | tf_op jit(solution)/shard_map/ppermute | solution.py:192
  142.4 28.2 %collective-permute-start = (f32[256,256]{0,1:T(8,128)S(1)}, f32[256,256]{0,1:T(8,128)S(1)}, u32[]{:S(2)}, u32[]{:S(2)}) collective-permute-start(f32[256,256]{0,1:T(8,128)S(1)} %get-tuple-element.136), channel_id=1, source_target_pairs={{1,0},{2,1},{3,2},{4,3},{5,4},{6,5},{7,6},{8,7},{9,8},{10,9},{11,1... | collective-permute-start | bytes 786440 | tf_op jit(solution)/shard_map/ppermute | solution.py:192
  167.0 54.3 %collective-permute-start.4 = (f32[256]{0:T(256)S(1)}, f32[256]{0:T(256)S(1)}, u32[]{:S(2)}, u32[]{:S(2)}) collective-permute-start(f32[256]{0:T(256)S(1)} %add.183), channel_id=1, source_target_pairs={{2,0},{3,1},{4,2},{5,3},{6,4},{7,5},{8,6},{9,7},{10,8},{11,9},{12,... | collective-permute-start | bytes 3080 | tf_op jit(solution)/shard_map/ppermute | solution.py:192
  169.4 57.7 %collective-permute-start.8 = (f32[256,256]{1,0:T(8,128)S(1)}, f32[256,256]{1,0:T(8,128)S(1)}, u32[]{:S(2)}, u32[]{:S(2)}) collective-permute-start(f32[256,256]{1,0:T(8,128)S(1)} %convolution_add_fusion.3), channel_id=1, source_target_pairs={{2,0},{3,1},{4,2},{5,3},{6,4},{7,5},{8,6},{9,7},{10,8},{11,9},{12,... | collective-permute-start | bytes 786440 | tf_op jit(solution)/shard_map/ppermute | solution.py:192
  171.3 58.6 %collective-permute-start.1 = (f32[256,256]{1,0:T(8,128)S(1)}, f32[256,256]{1,0:T(8,128)S(1)}, u32[]{:S(2)}, u32[]{:S(2)}) collective-permute-start(f32[256,256]{1,0:T(8,128)S(1)} %fusion.59), channel_id=1, source_target_pairs={{2,0},{3,1},{4,2},{5,3},{6,4},{7,5},{8,6},{9,7},{10,8},{11,9},{12,... | collective-permute-start | bytes 786440 | tf_op jit(solution)/shard_map/ppermute | solution.py:192
  221.6 99.9 %collective-permute-start.5 = (f32[256]{0:T(256)S(1)}, f32[256]{0:T(256)S(1)}, u32[]{:S(2)}, u32[]{:S(2)}) collective-permute-start(f32[256]{0:T(256)S(1)} %add.184), channel_id=1, source_target_pairs={{4,0},{5,1},{6,2},{7,3},{8,4},{9,5},{10,6},{11,7},{12,8},{13,9},{1... | collective-permute-start | bytes 3080 | tf_op jit(solution)/shard_map/ppermute | solution.py:192
  227.8 102.6 %collective-permute-start.9 = (f32[256,256]{1,0:T(8,128)S(1)}, f32[256,256]{1,0:T(8,128)S(1)}, u32[]{:S(2)}, u32[]{:S(2)}) collective-permute-start(f32[256,256]{1,0:T(8,128)S(1)} %convolution_add_fusion.2), channel_id=1, source_target_pairs={{4,0},{5,1},{6,2},{7,3},{8,4},{9,5},{10,6},{11,7},{12,8},{13,9},{1... | collective-permute-start | bytes 786440 | tf_op jit(solution)/shard_map/ppermute | solution.py:192
  230.2 103.1 %collective-permute-start.2 = (f32[256,256]{1,0:T(8,128)S(1)}, f32[256,256]{1,0:T(8,128)S(1)}, u32[]{:S(2)}, u32[]{:S(2)}) collective-permute-start(f32[256,256]{1,0:T(8,128)S(1)} %fusion.60), channel_id=1, source_target_pairs={{4,0},{5,1},{6,2},{7,3},{8,4},{9,5},{10,6},{11,7},{12,8},{13,9},{1... | collective-permute-start | bytes 786440 | tf_op jit(solution)/shard_map/ppermute | solution.py:192
  321.7 156.9 %collective-permute-start.6 = (f32[256]{0:T(256)S(1)}, f32[256]{0:T(256)S(1)}, u32[]{:S(2)}, u32[]{:S(2)}) collective-permute-start(f32[256]{0:T(256)S(1)} %add.185), channel_id=1, source_target_pairs={{8,0},{9,1},{10,2},{11,3},{12,4},{13,5},{14,6},{15,7},{24,16},{25,... | collective-permute-start | bytes 3080 | tf_op jit(solution)/shard_map/ppermute | solution.py:192
  331.3 165.3 %collective-permute-start.10 = (f32[256,256]{1,0:T(8,128)S(1)}, f32[256,256]{1,0:T(8,128)S(1)}, u32[]{:S(2)}, u32[]{:S(2)}) collective-permute-start(f32[256,256]{1,0:T(8,128)S(1)} %convolution_add_fusion.1), channel_id=1, source_target_pairs={{8,0},{9,1},{10,2},{11,3},{12,4},{13,5},{14,6},{15,7},{24,16},{25,... | collective-permute-start | bytes 786440 | tf_op jit(solution)/shard_map/ppermute | solution.py:192
where the time goes:
time: 505 us; the launch traced here: 498 us
  waiting for transfers between devices  336 us (67%)
  other arithmetic  100 us (20%)
  blocking collectives  23.1 us (5%)
  starting transfers between devices  16.2 us (3%)
  matrix products  12.2 us (2%)
  local copies, waits for them, and re-layouts  6.42 us (1%)
    ppermute x11, waiting for transfers between devices, shards(): received = lax.ppermute(running, 'tm', pairs)  336 us
    another operation x6, other arithmetic, smoother_elements(): factor = jnp.linalg.cholesky(predicted)  34 us
    another operation x6, other arithmetic, kalman_update(): factor = jnp.linalg.cholesky(normal)  24.9 us
    all_gather x1, blocking collectives, shards(): gathered = lax.all_gather(packed, 'tm', tiled=True)  23.1 us
    another operation x4, other arithmetic, kalman_update(): half = lax.linalg.triangular_solve(factor, rhs, left_side=True, lower=True)  20.9 us
    another operation x3, other arithmetic, smoother_elements(): lax.linalg.triangular_solve(factor, half_solve, left_side=True, lower=Tru...  19.7 us
    ppermute x11, starting transfers between devices, shards(): received = lax.ppermute(running, 'tm', pairs)  16.2 us
  transfers between devices with their start and end apart: 11, of which 9 were waited for; matrix products, arithmetic and copies ran while one was open for 1% of the time, Pallas kernels for 0%

commit v1 on v0

--- a/solution.py
+++ b/solution.py
@@ -118,7 +118,22 @@
     total_steps = tm_count * local_steps
     root_local = jnp.sqrt(obs_masks.astype(jnp.float32) / noise_var)
     packed = jnp.stack([observed, root_local], axis=1)
-    gathered = lax.all_gather(packed, "tm", tiled=True)
+    ways, here, k = (lax.axis_size("tm"), lax.axis_index("tm"), packed.shape[0])
+    dims = [n * ways if d == 0 else n for d, n in enumerate(packed.shape)]
+    gathered = lax.dynamic_update_slice_in_dim(
+        jnp.zeros(dims, packed.dtype), packed, here * k, axis=0
+    )
+    going_up = going_down = packed
+    for far in range(1, ways // 2 + 1):
+        going_up = lax.ppermute(going_up, "tm", [(d, (d + 1) % ways) for d in range(ways)])
+        gathered = lax.dynamic_update_slice_in_dim(
+            gathered, going_up, (here - far) % ways * k, axis=0
+        )
+        if 2 * far < ways:
+            going_down = lax.ppermute(going_down, "tm", [(d, (d - 1) % ways) for d in range(ways)])
+            gathered = lax.dynamic_update_slice_in_dim(
+                gathered, going_down, (here + far) % ways * k, axis=0
+            )
     obs_all = gathered[:, 0]
     root_all = gathered[:, 1]
     mean_first, cov_first = kalman_update(

time: 505 us -> 524 us (1.038)
  starting transfers between devices: 16.2 us -> 46.6 us
  blocking collectives: 23.1 us -> 0 us
  waiting for transfers between devices: 336 us -> 346 us
    ppermute x0 -> x15, starting transfers between devices: none -> 30.4 us  [the longest x7 24.2 us: shards(): lax.ppermute(going_down, 'tm', [(d, (d - 1) % ways) for d in range(ways)])]
    all_gather x1 -> x0, blocking collectives: 23.1 us -> none  [shards(): gathered = lax.all_gather(packed, 'tm', tiled=True)]
    ppermute x0 -> x15, waiting for transfers between devices: none -> 9.78 us  [the longest x8 8.11 us: shards(): lax.ppermute(going_up, 'tm', [(d, (d + 1) % ways) for d in range(ways)])]
  transfers between devices with their start and end apart: 11 -> 26, of which waited for: 9 -> 23; matrix products, arithmetic and copies ran while one was open for 1% -> 1% of each run, Pallas kernels for 0% -> 0%
where the time goes in v1:
time: 524 us; the launch traced here: 517 us
  waiting for transfers between devices  346 us (66%)
  other arithmetic  101 us (19%)
  starting transfers between devices  46.6 us (9%)
  matrix products  12.2 us (2%)
  local copies, waits for them, and re-layouts  7.04 us (1%)
    ppermute x11, waiting for transfers between devices, shards(): received = lax.ppermute(running, 'tm', pairs)  336 us
    another operation x6, other arithmetic, smoother_elements(): factor = jnp.linalg.cholesky(predicted)  34 us
    another operation x6, other arithmetic, kalman_update(): factor = jnp.linalg.cholesky(normal)  24.8 us
    ppermute x7, starting transfers between devices, shards(): lax.ppermute(going_down, 'tm', [(d, (d - 1) % ways) for d in range(ways)])  24.2 us
    another operation x4, other arithmetic, kalman_update(): half = lax.linalg.triangular_solve(factor, rhs, left_side=True, lower=True)  20.9 us
    another operation x3, other arithmetic, smoother_elements(): lax.linalg.triangular_solve(factor, half_solve, left_side=True, lower=Tru...  19.7 us
    ppermute x11, starting transfers between devices, shards(): received = lax.ppermute(running, 'tm', pairs)  16.2 us
  transfers between devices with their start and end apart: 26, of which 23 were waited for; matrix products, arithmetic and copies ran while one was open for 1% of the time, Pallas kernels for 0%

profile of v1, /device:TPU:1, one launch (start us, length us, event | category | flops | bytes accessed | tf_op | source)
XLA Modules:
  0.0 516.9 jit_solution(4608126561545654178)
XLA Ops:
  0.6 0.7 sqrt_bitcast_fusion
  2.0 2.6 collective-permute-start
  5.3 2.3 collective-permute-start.2
  7.9 0.9 collective-permute-start.3
  9.4 1.2 collective-permute-start.4
  10.9 3.6 collective-permute-start.5
  15.4 4.9 collective-permute-start.7
  21.0 4.9 collective-permute-start.9
  26.7 5.0 collective-permute-start.11
  32.5 4.9 collective-permute-start.13
  38.3 5.2 %collective-permute-done.14 = f32[1,2,128]{2,1,0:T(2,128)S(1)} collective-permute-done((f32[1,2,128]{2,1,0:T(2,128)S(1)}, f32[1,2,128]{2,1,0:T(2,128)S(1)}, u32[]{:S(2)}, u32[]{:S(2)}) %collective-permute-start.14) | collective-permute-done | bytes 1056 | tf_op jit(solution)/shard_map/ppermute | solution.py:128
  44.0 11.7 %custom-call.32 = f32[128,128]{1,0:T(8,128)S(1)} custom-call(f32[128,128]{1,0:T(8,128)S(1)} %fusion.49), custom_call_target="Cholesky" | custom-call | tf_op jit(solution)/shard_map/jit(cholesky)/cholesky/custom-call.1 | solution.py:77
  55.8 0.7 compare_reduce_fusion.3
  57.1 9.8 %custom-call.33 = f32[1,128,128]{1,2,0:T(8,128)S(1)} custom-call(f32[1,128,128]{2,1,0:T(8,128)S(1)} %fusion.47), custom_call_target="InvertDiagBlocksLowerTriangular" | custom-call | tf_op jit(solution)/shard_map/triangular_solve/custom-call.0 | solution.py:80
  68.2 24.9 %while.14 = (s32[]{:T(128)}, f32[256]{0:T(256)S(1)}, f32[256,256]{0,1:T(8,128)S(1)}, s32[]{:T(128)}, f32[128]{0:T(128)S(1)}, /*index=5*/f32[128]{0:T(128)S(1)}, ...) while((s32[]{:T(128)}, f32[256]{0:T(256)S(1)}, ...), condition=%wide.region_3.6_spmd, body=%wide.region_2.5_spmd.sunk | while | flops 152618752 | bytes 5461689 | solution.py:155
  69.2 11.7 %custom-call.37 = f32[128,128]{1,0:T(8,128)S(1)} custom-call(f32[128,128]{1,0:T(8,128)S(1)} %fusion.128), custom_call_target="Cholesky" | custom-call | tf_op jit(solution)/shard_map/while/body/jit(cholesky)/cholesky/custom-call.1 | solution.py:77
  82.2 9.8 %custom-call.38 = f32[1,128,128]{1,2,0:T(8,128)S(1)} custom-call(f32[1,128,128]{2,1,0:T(8,128)S(1)} %fusion.129), custom_call_target="InvertDiagBlocksLowerTriangular" | custom-call | tf_op jit(solution)/shard_map/while/body/triangular_solve/custom-call.0 | solution.py:80
  93.1 63.9 %conditional.1 = (f32[1,256]{1,0:T(1,128)S(1)}, f32[256,256]{0,1:T(8,128)S(1)}, f32[1,256,256]{2,1,0:T(8,128)S(1)}) conditional(s32[]{:T(128)} %convert_element_type.18, (f32[128]{0:T(128)S(1)}, f32[1,256,256]{1,2,0:T(8,128)S(1)}, f32[128]{0:T(128)S(1)}, f32[128]{0:T(128)S(1)}, f32[128]{0:T(128)S(1)}, /*index=5*/f32[256,256]{0,1:T(8,128)S(1)}, ...), branch_computations={%region_4.11_spmd, %region_9.12_spmd} | conditional | flops 556025344 | bytes 11482373 | solution.py:183
  94.2 11.7 %custom-call.24 = f32[1,128,128]{2,1,0:T(8,128)S(1)} custom-call(f32[1,128,128]{2,1,0:T(8,128)S(1)} %cholesky.48), custom_call_target="Cholesky" | custom-call | tf_op jit(solution)/shard_map/cond/branch_0_fun/jit(cholesky)/cholesky | solution.py:90
  106.0 9.8 %custom-call.25 = f32[1,1,128,128]{2,3,1,0:T(8,128)S(1)} custom-call(f32[1,1,128,128]{3,2,1,0:T(8,128)S(1)} %get-tuple-element.207), custom_call_target="InvertDiagBlocksLowerTriangular" | custom-call | tf_op jit(solution)/shard_map/cond/branch_0_fun/jit(cholesky)/cholesky | solution.py:90
  116.3 11.7 %custom-call.26 = f32[1,128,128]{2,1,0:T(8,128)S(1)} custom-call(f32[1,128,128]{2,1,0:T(8,128)S(1)} %fusion.20), custom_call_target="Cholesky" | custom-call | tf_op jit(solution)/shard_map/cond/branch_0_fun/jit(cholesky)/cholesky | solution.py:90
  128.0 0.7 compare_reduce_fusion.1
  130.1 4.1 while.13
  130.8 1.3 bitcast_dynamic-update-slice_fusion.3
  132.8 1.3 bitcast_dynamic-update-slice_fusion.3
  134.2 19.7 %custom-call.27 = f32[1,2,128,128]{2,3,1,0:T(8,128)S(1)} custom-call(f32[1,2,128,128]{3,2,1,0:T(8,128)S(1)} %bitcast.294), custom_call_target="InvertDiagBlocksLowerTriangular" | custom-call | tf_op jit(solution)/shard_map/cond/branch_0_fun/triangular_solve | solution.py:92
  157.0 1.9 collective-permute-start.22
  158.9 1.9 collective-permute-start.18
  160.8 1.9 collective-permute-start.15
  162.8 22.1 %collective-permute-done.18 = f32[256]{0:T(256)S(1)} collective-permute-done((f32[256]{0:T(256)S(1)}, f32[256]{0:T(256)S(1)}, u32[]{:S(2)}, u32[]{:S(2)}) %collective-permute-start.18) | collective-permute-done | bytes 1056 | tf_op jit(solution)/shard_map/ppermute | solution.py:207
  185.1 1.3 collective-permute-start.19
  187.4 1.3 collective-permute-start.23
  189.4 1.3 collective-permute-start.16
  190.7 42.7 %collective-permute-done.19 = f32[256]{0:T(256)S(1)} collective-permute-done((f32[256]{0:T(256)S(1)}, f32[256]{0:T(256)S(1)}, u32[]{:S(2)}, u32[]{:S(2)}) %collective-permute-start.19) | collective-permute-done | bytes 1056 | tf_op jit(solution)/shard_map/ppermute | solution.py:207
  233.7 1.3 collective-permute-start.20
  235.0 4.1 collective-permute-done.23
  239.9 1.3 collective-permute-start.24
  241.2 0.7 collective-permute-done.16
  242.3 1.3 collective-permute-start.17
  243.6 92.7 %collective-permute-done.20 = f32[256]{0:T(256)S(1)} collective-permute-done((f32[256]{0:T(256)S(1)}, f32[256]{0:T(256)S(1)}, u32[]{:S(2)}, u32[]{:S(2)}) %collective-permute-start.20) | collective-permute-done | bytes 1056 | tf_op jit(solution)/shard_map/ppermute | solution.py:207
  336.6 1.3 collective-permute-start.21
  337.9 7.4 %collective-permute-done.24 = f32[256,256]{1,0:T(8,128)S(1)} collective-permute-done((f32[256,256]{1,0:T(8,128)S(1)}, f32[256,256]{1,0:T(8,128)S(1)}, u32[]{:S(2)}, u32[]{:S(2)}) %collective-permute-start.24) | collective-permute-done | bytes 262176 | tf_op jit(solution)/shard_map/ppermute | solution.py:207
  346.1 1.3 collective-permute-start.25
  347.4 0.7 collective-permute-done.17
  348.5 148.8 %collective-permute-done.21 = f32[256]{0:T(256)S(1)} collective-permute-done((f32[256]{0:T(256)S(1)}, f32[256]{0:T(256)S(1)}, u32[]{:S(2)}, u32[]{:S(2)}) %collective-permute-start.21) | collective-permute-done | bytes 1056 | tf_op jit(solution)/shard_map/ppermute | solution.py:207
  497.3 0.9 convolution_add_fusion.4
  498.2 17.0 %collective-permute-done.25 = f32[256,256]{1,0:T(8,128)S(1)} collective-permute-done((f32[256,256]{1,0:T(8,128)S(1)}, f32[256,256]{1,0:T(8,128)S(1)}, u32[]{:S(2)}, u32[]{:S(2)}) %collective-permute-start.25) | collective-permute-done | bytes 262176 | tf_op jit(solution)/shard_map/ppermute | solution.py:207
  515.6 1.1 fusion.38
  (133 shorter events, 22.1 us)
Async XLA Ops:
  1.3 0.7 copy-start.1
  2.0 3.4 collective-permute-start
  4.6 3.3 collective-permute-start.1
  4.6 0.7 copy-start.2
  5.3 4.0 collective-permute-start.2
  7.6 18.8 %copy-start = (f32[128,128]{1,0:T(8,128)S(1)}, f32[128,128]{1,0:T(8,128)}, u32[]{:S(2)}) copy-start(f32[128,128]{1,0:T(8,128)} %param.16) | copy-start | bytes 196612
  7.9 3.0 collective-permute-start.3
  9.4 5.7 %collective-permute-start.4 = (f32[1,2,128]{2,1,0:T(2,128)S(1)}, f32[1,2,128]{2,1,0:T(2,128)S(1)}, u32[]{:S(2)}, u32[]{:S(2)}) collective-permute-start(f32[1,2,128]{2,1,0:T(2,128)S(1)} %collective-permute-done.2), channel_id=1, source_target_pairs={{0,1},{1,2},{2,3},{3,4},{4,5},{5,6},{6,7},{7,8},{8,9},{9,10},{10,1... | collective-permute-start | bytes 3080 | tf_op jit(solution)/shard_map/ppermute | solution.py:128
  10.9 4.5 collective-permute-start.5
  15.1 5.7 %collective-permute-start.6 = (f32[1,2,128]{2,1,0:T(2,128)S(1)}, f32[1,2,128]{2,1,0:T(2,128)S(1)}, u32[]{:S(2)}, u32[]{:S(2)}) collective-permute-start(f32[1,2,128]{2,1,0:T(2,128)S(1)} %collective-permute-done.4), channel_id=1, source_target_pairs={{0,1},{1,2},{2,3},{3,4},{4,5},{5,6},{6,7},{7,8},{8,9},{9,10},{10,1... | collective-permute-start | bytes 3080 | tf_op jit(solution)/shard_map/ppermute | solution.py:128
  15.4 5.7 %collective-permute-start.7 = (f32[1,2,128]{2,1,0:T(2,128)S(1)}, f32[1,2,128]{2,1,0:T(2,128)S(1)}, u32[]{:S(2)}, u32[]{:S(2)}) collective-permute-start(f32[1,2,128]{2,1,0:T(2,128)S(1)} %collective-permute-done.5), channel_id=1, source_target_pairs={{0,15},{1,0},{2,1},{3,2},{4,3},{5,4},{6,5},{7,6},{8,7},{9,8},{10,9... | collective-permute-start | bytes 3080 | tf_op jit(solution)/shard_map/ppermute | solution.py:133
  20.8 5.7 %collective-permute-start.8 = (f32[1,2,128]{2,1,0:T(2,128)S(1)}, f32[1,2,128]{2,1,0:T(2,128)S(1)}, u32[]{:S(2)}, u32[]{:S(2)}) collective-permute-start(f32[1,2,128]{2,1,0:T(2,128)S(1)} %collective-permute-done.6), channel_id=1, source_target_pairs={{0,1},{1,2},{2,3},{3,4},{4,5},{5,6},{6,7},{7,8},{8,9},{9,10},{10,1... | collective-permute-start | bytes 3080 | tf_op jit(solution)/shard_map/ppermute | solution.py:128
  21.0 5.7 %collective-permute-start.9 = (f32[1,2,128]{2,1,0:T(2,128)S(1)}, f32[1,2,128]{2,1,0:T(2,128)S(1)}, u32[]{:S(2)}, u32[]{:S(2)}) collective-permute-start(f32[1,2,128]{2,1,0:T(2,128)S(1)} %collective-permute-done.7), channel_id=1, source_target_pairs={{0,15},{1,0},{2,1},{3,2},{4,3},{5,4},{6,5},{7,6},{8,7},{9,8},{10,9... | collective-permute-start | bytes 3080 | tf_op jit(solution)/shard_map/ppermute | solution.py:133
  26.4 5.7 %collective-permute-start.10 = (f32[1,2,128]{2,1,0:T(2,128)S(1)}, f32[1,2,128]{2,1,0:T(2,128)S(1)}, u32[]{:S(2)}, u32[]{:S(2)}) collective-permute-start(f32[1,2,128]{2,1,0:T(2,128)S(1)} %collective-permute-done.8), channel_id=1, source_target_pairs={{0,1},{1,2},{2,3},{3,4},{4,5},{5,6},{6,7},{7,8},{8,9},{9,10},{10,1... | collective-permute-start | bytes 3080 | tf_op jit(solution)/shard_map/ppermute | solution.py:128
  26.7 5.8 %collective-permute-start.11 = (f32[1,2,128]{2,1,0:T(2,128)S(1)}, f32[1,2,128]{2,1,0:T(2,128)S(1)}, u32[]{:S(2)}, u32[]{:S(2)}) collective-permute-start(f32[1,2,128]{2,1,0:T(2,128)S(1)} %collective-permute-done.9), channel_id=1, source_target_pairs={{0,15},{1,0},{2,1},{3,2},{4,3},{5,4},{6,5},{7,6},{8,7},{9,8},{10,9... | collective-permute-start | bytes 3080 | tf_op jit(solution)/shard_map/ppermute | solution.py:133
  32.1 5.7 %collective-permute-start.12 = (f32[1,2,128]{2,1,0:T(2,128)S(1)}, f32[1,2,128]{2,1,0:T(2,128)S(1)}, u32[]{:S(2)}, u32[]{:S(2)}) collective-permute-start(f32[1,2,128]{2,1,0:T(2,128)S(1)} %collective-permute-done.10), channel_id=1, source_target_pairs={{0,1},{1,2},{2,3},{3,4},{4,5},{5,6},{6,7},{7,8},{8,9},{9,10},{10,1... | collective-permute-start | bytes 3080 | tf_op jit(solution)/shard_map/ppermute | solution.py:128
  32.5 5.7 %collective-permute-start.13 = (f32[1,2,128]{2,1,0:T(2,128)S(1)}, f32[1,2,128]{2,1,0:T(2,128)S(1)}, u32[]{:S(2)}, u32[]{:S(2)}) collective-permute-start(f32[1,2,128]{2,1,0:T(2,128)S(1)} %collective-permute-done.11), channel_id=1, source_target_pairs={{0,15},{1,0},{2,1},{3,2},{4,3},{5,4},{6,5},{7,6},{8,7},{9,8},{10,9... | collective-permute-start | bytes 3080 | tf_op jit(solution)/shard_map/ppermute | solution.py:133
  37.8 5.7 %collective-permute-start.14 = (f32[1,2,128]{2,1,0:T(2,128)S(1)}, f32[1,2,128]{2,1,0:T(2,128)S(1)}, u32[]{:S(2)}, u32[]{:S(2)}) collective-permute-start(f32[1,2,128]{2,1,0:T(2,128)S(1)} %collective-permute-done.12), channel_id=1, source_target_pairs={{0,1},{1,2},{2,3},{3,4},{4,5},{5,6},{6,7},{7,8},{8,9},{9,10},{10,1... | collective-permute-start | bytes 3080 | tf_op jit(solution)/shard_map/ppermute | solution.py:128
  157.0 29.5 %collective-permute-start.22 = (f32[256,256]{1,0:T(8,128)S(1)}, f32[256,256]{1,0:T(8,128)S(1)}, u32[]{:S(2)}, u32[]{:S(2)}) collective-permute-start(f32[256,256]{1,0:T(8,128)S(1)} %bitcast.260), channel_id=1, source_target_pairs={{1,0},{2,1},{3,2},{4,3},{5,4},{6,5},{7,6},{8,7},{9,8},{10,9},{11,1... | collective-permute-start | bytes 786440 | tf_op jit(solution)/shard_map/ppermute | solution.py:207
  158.9 26.0 %collective-permute-start.18 = (f32[256]{0:T(256)S(1)}, f32[256]{0:T(256)S(1)}, u32[]{:S(2)}, u32[]{:S(2)}) collective-permute-start(f32[256]{0:T(256)S(1)} %bitcast.271), channel_id=1, source_target_pairs={{1,0},{2,1},{3,2},{4,3},{5,4},{6,5},{7,6},{8,7},{9,8},{10,9},{11,1... | collective-permute-start | bytes 3080 | tf_op jit(solution)/shard_map/ppermute | solution.py:207
  160.8 27.9 %collective-permute-start.15 = (f32[256,256]{0,1:T(8,128)S(1)}, f32[256,256]{0,1:T(8,128)S(1)}, u32[]{:S(2)}, u32[]{:S(2)}) collective-permute-start(f32[256,256]{0,1:T(8,128)S(1)} %get-tuple-element.136), channel_id=1, source_target_pairs={{1,0},{2,1},{3,2},{4,3},{5,4},{6,5},{7,6},{8,7},{9,8},{10,9},{11,1... | collective-permute-start | bytes 786440 | tf_op jit(solution)/shard_map/ppermute | solution.py:207
  185.1 48.3 %collective-permute-start.19 = (f32[256]{0:T(256)S(1)}, f32[256]{0:T(256)S(1)}, u32[]{:S(2)}, u32[]{:S(2)}) collective-permute-start(f32[256]{0:T(256)S(1)} %add.341), channel_id=1, source_target_pairs={{2,0},{3,1},{4,2},{5,3},{6,4},{7,5},{8,6},{9,7},{10,8},{11,9},{12,... | collective-permute-start | bytes 3080 | tf_op jit(solution)/shard_map/ppermute | solution.py:207
  187.4 51.7 %collective-permute-start.23 = (f32[256,256]{1,0:T(8,128)S(1)}, f32[256,256]{1,0:T(8,128)S(1)}, u32[]{:S(2)}, u32[]{:S(2)}) collective-permute-start(f32[256,256]{1,0:T(8,128)S(1)} %convolution_add_fusion.3), channel_id=1, source_target_pairs={{2,0},{3,1},{4,2},{5,3},{6,4},{7,5},{8,6},{9,7},{10,8},{11,9},{12,... | collective-permute-start | bytes 786440 | tf_op jit(solution)/shard_map/ppermute | solution.py:207
  189.4 52.6 %collective-permute-start.16 = (f32[256,256]{1,0:T(8,128)S(1)}, f32[256,256]{1,0:T(8,128)S(1)}, u32[]{:S(2)}, u32[]{:S(2)}) collective-permute-start(f32[256,256]{1,0:T(8,128)S(1)} %fusion.58), channel_id=1, source_target_pairs={{2,0},{3,1},{4,2},{5,3},{6,4},{7,5},{8,6},{9,7},{10,8},{11,9},{12,... | collective-permute-start | bytes 786440 | tf_op jit(solution)/shard_map/ppermute | solution.py:207
  233.7 102.6 %collective-permute-start.20 = (f32[256]{0:T(256)S(1)}, f32[256]{0:T(256)S(1)}, u32[]{:S(2)}, u32[]{:S(2)}) collective-permute-start(f32[256]{0:T(256)S(1)} %add.342), channel_id=1, source_target_pairs={{4,0},{5,1},{6,2},{7,3},{8,4},{9,5},{10,6},{11,7},{12,8},{13,9},{1... | collective-permute-start | bytes 3080 | tf_op jit(solution)/shard_map/ppermute | solution.py:207
  239.9 105.4 %collective-permute-start.24 = (f32[256,256]{1,0:T(8,128)S(1)}, f32[256,256]{1,0:T(8,128)S(1)}, u32[]{:S(2)}, u32[]{:S(2)}) collective-permute-start(f32[256,256]{1,0:T(8,128)S(1)} %convolution_add_fusion.2), channel_id=1, source_target_pairs={{4,0},{5,1},{6,2},{7,3},{8,4},{9,5},{10,6},{11,7},{12,8},{13,9},{1... | collective-permute-start | bytes 786440 | tf_op jit(solution)/shard_map/ppermute | solution.py:207
  242.3 105.8 %collective-permute-start.17 = (f32[256,256]{1,0:T(8,128)S(1)}, f32[256,256]{1,0:T(8,128)S(1)}, u32[]{:S(2)}, u32[]{:S(2)}) collective-permute-start(f32[256,256]{1,0:T(8,128)S(1)} %fusion.59), channel_id=1, source_target_pairs={{4,0},{5,1},{6,2},{7,3},{8,4},{9,5},{10,6},{11,7},{12,8},{13,9},{1... | collective-permute-start | bytes 786440 | tf_op jit(solution)/shard_map/ppermute | solution.py:207
  336.6 160.8 %collective-permute-start.21 = (f32[256]{0:T(256)S(1)}, f32[256]{0:T(256)S(1)}, u32[]{:S(2)}, u32[]{:S(2)}) collective-permute-start(f32[256]{0:T(256)S(1)} %add.343), channel_id=1, source_target_pairs={{8,0},{9,1},{10,2},{11,3},{12,4},{13,5},{14,6},{15,7},{24,16},{25,... | collective-permute-start | bytes 3080 | tf_op jit(solution)/shard_map/ppermute | solution.py:207
  346.1 169.1 %collective-permute-start.25 = (f32[256,256]{1,0:T(8,128)S(1)}, f32[256,256]{1,0:T(8,128)S(1)}, u32[]{:S(2)}, u32[]{:S(2)}) collective-permute-start(f32[256,256]{1,0:T(8,128)S(1)} %convolution_add_fusion.1), channel_id=1, source_target_pairs={{8,0},{9,1},{10,2},{11,3},{12,4},{13,5},{14,6},{15,7},{24,16},{25,... | collective-permute-start | bytes 786440 | tf_op jit(solution)/shard_map/ppermute | solution.py:207
